TPU v7x, 256 devices: a whole 4x4x8 slice. The times are simulated.
256 devices in a mesh: samp: 64 (over x, z, core), blk: 4 (over y).
Axes of the slice: x: 4, y: 4, z: 8, core: 2. Of those that a mesh axis runs over, the one named last changes fastest.
Arguments:
- dosages: bfloat16 [40960, 2048], P('samp', 'blk'), may hold values from 0 to 2
- traits: bfloat16 [16, 40960], P(None, 'samp'), may hold values from -6 to 6
- folds: int32 [40960], P('samp'), may hold values from 0 to 4
Outputs:
- level0: float32 [4, 5, 16, 40960], P(None, None, 'blk', 'samp')
- blend: float32 [16, 40960], P('blk', 'samp')
All inputs are finite; a program needn't handle non-finite values.
Results may differ from a plain program's by a relative error of at most 0.0097.
Values may be sent and summed in bfloat16 or wider, within the bound.
No kernel may reach another device: no remote copies, remote signals or barrier semaphores. Data moves between devices by JAX's collectives and lax.ppermute only.
A program may use at most 64 MiB of HBM per device.

v0:
```python
import jax
import jax.numpy as jnp
from jax import lax
from jax.sharding import PartitionSpec as P

FOLDS = 5
SHRINK = 5
RATIOS = (99.0, 3.0, 1.0, 1.0 / 3.0, 1.0 / 99.0)
EPS = 1e-05
HIGH = lax.Precision.HIGHEST


def solve_batch(systems, right_sides):
    factors = jnp.linalg.cholesky(systems)

    def solve_single(factor, right_side):
        return jax.scipy.linalg.cho_solve((factor, True), right_side)

    return jax.vmap(solve_single)(factors, right_sides)


def shards(dosages, traits, folds):
    rows, width = dosages.shape
    traits_count = traits.shape[0]
    fold_ids = jnp.arange(FOLDS, dtype=jnp.int32)
    masks = (folds[None, :] == fold_ids[:, None]).astype(jnp.float32)
    mask_half = masks.astype(jnp.bfloat16)
    traits_wide = traits.astype(jnp.float32)
    grams = []
    crosses = []
    for fold in range(FOLDS):
        weighted = dosages * mask_half[fold][:, None]
        grams.append(jnp.einsum("ri,rj->ij", dosages, weighted, preferred_element_type=jnp.float32))
        crosses.append(
            jnp.dot(traits * mask_half[fold][None, :], dosages, preferred_element_type=jnp.float32)
        )
    gram = jnp.stack(grams)
    cross = jnp.stack(crosses)
    sums = jnp.dot(mask_half, dosages, preferred_element_type=jnp.float32)
    counts = jnp.sum(masks, axis=1)
    trait_sums = jnp.einsum("ks,ts->kt", masks, traits_wide, precision=HIGH)
    gram, sums, cross, counts, trait_sums = lax.psum(
        (gram, sums, cross, counts, trait_sums), "samp"
    )
    total = jnp.sum(counts)
    mean = jnp.sum(sums, axis=0) / total
    gram_total = jnp.sum(gram, axis=0)
    variance = jnp.diagonal(gram_total) / total - mean * mean
    scale = lax.rsqrt(variance + EPS)
    sums_total = jnp.sum(sums, axis=0)
    cross_total = jnp.sum(cross, axis=0)
    trait_total = jnp.sum(trait_sums, axis=0)
    ratios = jnp.array(RATIOS, dtype=jnp.float32)
    identity = jnp.eye(width, dtype=jnp.float32)

    def train_system(fold):
        train_gram = gram_total - lax.dynamic_index_in_dim(gram, fold, 0, keepdims=False)
        train_sums = sums_total - lax.dynamic_index_in_dim(sums, fold, 0, keepdims=False)
        train_count = total - lax.dynamic_index_in_dim(counts, fold, 0, keepdims=False)
        train_cross = cross_total - lax.dynamic_index_in_dim(cross, fold, 0, keepdims=False)
        train_traits = trait_total - lax.dynamic_index_in_dim(trait_sums, fold, 0, keepdims=False)
        centered = (
            train_gram
            - mean[:, None] * train_sums[None, :]
            - train_sums[:, None] * mean[None, :]
            + train_count * mean[:, None] * mean[None, :]
        )
        system = scale[:, None] * centered * scale[None, :]
        target = scale[:, None] * (train_cross.T - mean[:, None] * train_traits[None, :])
        return (system, target)

    systems_count = FOLDS * SHRINK
    per_device = -(-systems_count // lax.axis_size("samp"))
    first = lax.axis_index("samp") * per_device

    def solve_own(offset):
        which = jnp.minimum(first + offset, systems_count - 1)
        fold = which // SHRINK
        shrink = which - fold * SHRINK
        system, target = train_system(fold)
        penalty = jnp.sum(
            jnp.where(jnp.arange(SHRINK, dtype=jnp.int32) == shrink, ratios * width, 0.0)
        )
        beta = solve_batch((system + penalty * identity)[None], target[None])[0]
        return (scale[:, None] * beta).astype(jnp.bfloat16)

    owned = lax.map(solve_own, jnp.arange(per_device, dtype=jnp.int32))
    collected = lax.all_gather(owned, "samp", axis=0, tiled=True)
    coef = collected[:systems_count].reshape(FOLDS, SHRINK, width, traits_count)
    coef_flat = coef.transpose(2, 0, 1, 3).reshape(width, FOLDS * SHRINK * traits_count)
    shift = jnp.einsum("v,klvt->klt", mean, coef.astype(jnp.float32), precision=HIGH)
    raw = jnp.einsum("vc,rv->cr", coef_flat, dosages, preferred_element_type=jnp.float32)
    outcome = raw.reshape(FOLDS, SHRINK, traits_count, rows) - shift[..., None]
    level_pred = jnp.einsum("kltr,kr->ltr", outcome, masks, precision=HIGH)
    group = traits_count // lax.axis_size("blk")
    start = lax.axis_index("blk") * group
    own_traits = lax.dynamic_slice_in_dim(traits_wide, start, group, 0)
    moment_sum, moment_sq = lax.psum(
        (jnp.sum(level_pred, axis=-1), jnp.sum(level_pred * level_pred, axis=-1)), "samp"
    )
    pred_mean = moment_sum / total
    pred_var = moment_sq / total - pred_mean * pred_mean
    moved = (level_pred - pred_mean[..., None]) * lax.rsqrt(pred_var + EPS)[..., None]
    arrived = lax.all_to_all(moved[None], "blk", split_axis=2, concat_axis=0, tiled=True)
    count_pred = arrived.shape[0] * arrived.shape[1]
    flat = arrived.reshape(count_pred, group, rows)
    fold_grams = jnp.einsum("ks,ats,bts->ktab", masks, flat, flat, precision=HIGH)
    fold_cross = jnp.einsum("ks,ats,ts->kta", masks, flat, own_traits, precision=HIGH)
    fold_grams, fold_cross = lax.psum((fold_grams, fold_cross), "samp")
    level0 = flat.reshape(arrived.shape)
    train_grams = jnp.sum(fold_grams, axis=0)[None] - fold_grams
    train_cross = jnp.sum(fold_cross, axis=0)[None] - fold_cross
    shrunk = train_grams + total / 4.0 * jnp.eye(count_pred, dtype=jnp.float32)
    weights = solve_batch(
        shrunk.reshape(-1, count_pred, count_pred), train_cross.reshape(-1, count_pred)
    )
    weights = weights.reshape(FOLDS, group, count_pred)
    every_fold = jnp.einsum("ats,kta->kts", flat, weights, precision=HIGH)
    blended = jnp.einsum("kts,ks->ts", every_fold, masks, precision=HIGH)
    blend_sum, blend_sq = lax.psum(
        (jnp.sum(blended, axis=-1), jnp.sum(blended * blended, axis=-1)), "samp"
    )
    blend_mean = blend_sum / total
    blend_var = blend_sq / total - blend_mean * blend_mean
    blend = (blended - blend_mean[:, None]) * lax.rsqrt(blend_var + EPS)[:, None]
    return (level0, blend)


def solution(mesh):
    in_specs = (P("samp", "blk"), P(None, "samp"), P("samp"))
    out_specs = (P(None, None, "blk", "samp"), P("blk", "samp"))
    return jax.shard_map(shards, mesh=mesh, in_specs=in_specs, out_specs=out_specs, check_vma=False)
```

profile of v0, /device:TPU:1, one launch (start us, length us, event | category | flops | bytes accessed | tf_op | source)
XLA Modules:
  0.0 1099.6 jit_solution(9628487864287836600)
XLA Ops:
  7.2 0.8 convert_bitcast_fusion
  8.0 3.0 fusion.4
  11.0 1.3 fusion.25
  12.3 3.0 fusion.3
  15.5 1.7 fusion.2
  17.4 1.8 fusion.1
  19.3 1.7 fusion
  21.2 0.7 copy-done.5
  22.5 250.1 %all-reduce.4 = (f32[5,512]{1,0:T(8,128)S(1)}, f32[5]{0:T(128)S(1)}, f32[5,16]{1,0:T(8,128)S(1)}) all-reduce(f32[5,512]{1,0:T(8,128)S(1)} %fusion.107, f32[5]{0:T(128)S(1)} %convert_reduce_fusion, f32[5,16]{1,0:T(8,128)S(1)} %fusion.91), channel_id=1, replica_groups=mesh['samp'=64,'blk'=4] {'samp'}, use_global_device_ids=true, to_apply=%region_5.0 | all-reduce | flops 2645 | bytes 21160 | tf_op jit(solution)/shard_map/psum | solution.py:42
  275.0 0.6 fusion.108
  276.2 3.3 reduce_sum.128
  279.5 5.0 gather_fusion
  285.1 2.3 fusion.38
  288.0 1.0 copy-done.2
  289.0 11.7 %custom-call.57 = f32[1,128,128]{2,1,0:T(8,128)S(1)} custom-call(f32[1,128,128]{2,1,0:T(8,128)S(1)} %cholesky.302), custom_call_target="Cholesky" | custom-call | tf_op jit(solution)/shard_map/while/body/eval_jaxpr/jit(cholesky)/cholesky | solution.py:14
  300.8 9.8 custom-call.58
  310.7 1.2 fusion.64
  312.0 1.2 fusion.14
  313.3 11.7 %custom-call.59 = f32[1,128,128]{2,1,0:T(8,128)S(1)} custom-call(f32[1,128,128]{2,1,0:T(8,128)S(1)} %cholesky.306), custom_call_target="Cholesky" | custom-call | tf_op jit(solution)/shard_map/while/body/eval_jaxpr/jit(cholesky)/cholesky | solution.py:14
  325.3 10.0 custom-call.60
  335.6 1.5 fusion.16
  337.1 11.7 %custom-call.61 = f32[1,128,128]{2,1,0:T(8,128)S(1)} custom-call(f32[1,128,128]{2,1,0:T(8,128)S(1)} %cholesky.311), custom_call_target="Cholesky" | custom-call | tf_op jit(solution)/shard_map/while/body/eval_jaxpr/jit(cholesky)/cholesky | solution.py:14
  349.0 9.8 custom-call.62
  359.1 1.3 fusion.19
  360.4 11.9 %custom-call.63 = f32[1,128,128]{2,1,0:T(8,128)S(1)} custom-call(f32[1,128,128]{2,1,0:T(8,128)S(1)} %fusion.19), custom_call_target="Cholesky" | custom-call | tf_op jit(solution)/shard_map/while/body/eval_jaxpr/jit(cholesky)/cholesky | solution.py:14
  372.5 0.7 compare_reduce_fusion.2
  373.2 0.6 compare_reduce_fusion.1
  373.8 0.7 compare_reduce_fusion.3
  377.2 8.9 while.1
  377.9 1.4 constant_dynamic-slice_fusion.8
  380.1 1.4 constant_dynamic-slice_fusion.8
  382.3 1.4 constant_dynamic-slice_fusion.8
  384.6 1.4 constant_dynamic-slice_fusion.8
  386.1 39.3 %custom-call.64 = f32[1,4,128,128]{2,3,1,0:T(8,128)S(1)} custom-call(f32[1,4,128,128]{3,2,1,0:T(8,128)S(1)} %bitcast.390), custom_call_target="InvertDiagBlocksLowerTriangular" | custom-call | tf_op jit(solution)/shard_map/while/body/eval_jaxpr/vmap(jit(_cho_solve))/triangular_solve | solution.py:17
  428.5 0.7 fusion.73
  429.2 76.2 %all-gather.2.cloned.1.call-done = bf16[64,512,16]{1,2,0:T(8,128)(2,1)} async-done(((bf16[1,512,16]{1,2,0:T(8,128)(2,1)}), bf16[64,512,16]{1,2,0:T(8,128)(2,1)}) %all-gather.2.cloned.1.call-update) | async-done | bytes 1048592 | tf_op jit(solution)/shard_map/all_gather | solution.py:88
  505.4 1.0 slice.254
  506.4 1.5 fusion.118
  508.5 125.7 %all-reduce.3 = (f32[5,16]{1,0:T(8,128)S(1)}, f32[5,16]{1,0:T(8,128)S(1)}) all-reduce(f32[5,16]{1,0:T(8,128)S(1)} %get-tuple-element.90, f32[5,16]{1,0:T(8,128)S(1)} %get-tuple-element.89), channel_id=1, replica_groups=mesh['samp'=64,'blk'=4] {'samp'}, use_global_device_ids=true, to_apply=%region_23.24 | all-reduce | flops 160 | bytes 1280 | tf_op jit(solution)/shard_map/psum | solution.py:98
  634.9 0.9 copy.84
  635.8 4.0 all-to-all-start
  640.4 4.6 all-to-all-done
  645.7 1.4 fusion.11
  647.1 245.2 %all-reduce.2 = (f32[5,4,20,20]{3,2,0,1:T(8,128)S(1)}, f32[5,4,20]{2,0,1:T(8,128)S(1)}) all-reduce(f32[5,4,20,20]{3,2,0,1:T(8,128)S(1)} %fusion.11, f32[5,4,20]{2,0,1:T(8,128)S(1)} %fusion.59), channel_id=1, replica_groups=mesh['samp'=64,'blk'=4] {'samp'}, use_global_device_ids=true, to_apply=%region_24.25 | all-reduce | flops 8400 | bytes 67200 | tf_op jit(solution)/shard_map/psum | solution.py:109
  892.9 36.7 %custom-call.65 = f32[20,20,20]{2,1,0:T(8,128)S(1)} custom-call(f32[20,20,20]{2,1,0:T(8,128)S(1)} %fusion.52), custom_call_target="Cholesky" | custom-call | tf_op jit(solution)/shard_map/jit(cholesky)/cholesky | solution.py:14
  929.8 30.9 %custom-call.66 = f32[20,1,20,20]{2,3,1,0:T(8,128)S(1)} custom-call(f32[20,1,20,20]{3,2,1,0:T(8,128)S(1)} %select_bitcast_fusion), custom_call_target="InvertDiagBlocksLowerTriangular" | custom-call | tf_op jit(solution)/shard_map/vmap(jit(_cho_solve))/triangular_solve | solution.py:17
  962.2 129.1 %all-reduce.1 = (f32[4]{0:T(128)S(1)}, f32[4]{0:T(128)S(1)}) all-reduce(f32[4]{0:T(128)S(1)} %get-tuple-element.92, f32[4]{0:T(128)S(1)} %get-tuple-element.91), channel_id=1, replica_groups=mesh['samp'=64,'blk'=4] {'samp'}, use_global_device_ids=true, to_apply=%region_31.32 | all-reduce | flops 8 | bytes 64 | tf_op jit(solution)/shard_map/psum | solution.py:120
  1091.8 0.7 multiply_bitcast_fusion.1
  (126 shorter events, 16.8 us)
Async XLA Ops:
  7.2 8.1 copy-start
  7.2 8.1 copy-start.3
  7.2 269.0 %all-reduce.8.cloned.1.call-start = ((), (), s32[]{:S(2)}) async-start(), calls=%async_computation.2 | async-start | bytes 10813440 | tf_op jit(solution)/shard_map/psum | solution.py:42
  19.1 2.9 copy-start.6
  19.2 255.8 %copy-start.7 = (f32[5]{0:T(128)S(1)}, f32[5]{0:T(128)}, u32[]{:S(2)}) copy-start(f32[5]{0:T(128)} %constant.327) | copy-start | bytes 64
  21.2 0.7 copy-start.5
  21.9 483.5 %all-gather.2.cloned.1.call-start = ((), (), s32[]{:S(2)}) async-start(), calls=%async_computation.1 | async-start | bytes 1064960 | tf_op jit(solution)/shard_map/all_gather | solution.py:88
  288.0 1.0 copy-start.2
  289.0 136.5 %copy-start.4 = (f32[5,16,512]{2,1,0:T(8,128)S(1)}, f32[5,16,512]{2,1,0:T(8,128)}, u32[]{:S(2)}) copy-start(f32[5,16,512]{2,1,0:T(8,128)} %get-tuple-element.116) | copy-start | bytes 491524
  635.8 9.2 all-to-all-start
  645.2 447.3 %copy-start.1 = (f32[4,1,5,4,640]{4,3,2,0,1:T(4,128)}, f32[4,1,5,4,640]{4,3,2,0,1:T(4,128)S(1)}, u32[]{:S(2)}) copy-start(f32[4,1,5,4,640]{4,3,2,0,1:T(4,128)S(1)} %copy.142) | copy-start | bytes 614404
Sparse Core Ops, SparseCore 0:
  22.0 201.1 all-reduce.7
  429.3 76.0 all-gather.1
where the time goes:
time: 1100 us
  blocking collectives  750 us (68%)
  other arithmetic  198 us (18%)
  waiting for transfers between devices  80.8 us (7%)
  matrix products  27.3 us (2%)
  local copies, waits for them, and re-layouts  19.7 us (2%)
  between operations  19.1 us (2%)
    psum x1, blocking collectives, shards(): lax.psum((gram, sums, cross, counts, trait_sums), 'samp')  250 us
    psum x1, blocking collectives, shards(): fold_grams, fold_cross = lax.psum((fold_grams, fold_cross), 'samp')  245 us
    psum x1, blocking collectives, shards(): lax.psum((jnp.sum(blended, axis=-1), jnp.sum(blended * blended, axis=-1))...  129 us
    psum x1, blocking collectives, shards(): lax.psum((jnp.sum(level_pred, axis=-1), jnp.sum(level_pred * level_pred,...  126 us
    another operation x18, other arithmetic, solve_batch(): factors = jnp.linalg.cholesky(systems)  116 us
    all_gather x1, waiting for transfers between devices, shards(): collected = lax.all_gather(owned, 'samp', axis=0, tiled=True)  76.2 us
    another operation x6, other arithmetic, solve_single(): return jax.scipy.linalg.cho_solve((factor, True), right_side)  70.5 us
  transfers between devices with their start and end apart: 3, of which 2 were waited for; matrix products, arithmetic and copies ran while one was open for 0% of the time, Pallas kernels for 0%

commit v1 on v0

--- a/solution.py
+++ b/solution.py
@@ -85,7 +85,9 @@
         return (scale[:, None] * beta).astype(jnp.bfloat16)
 
     owned = lax.map(solve_own, jnp.arange(per_device, dtype=jnp.int32))
-    collected = lax.all_gather(owned, "samp", axis=0, tiled=True)
+    collected = jnp.concatenate(
+        lax.all_to_all(jnp.stack([owned] * lax.axis_size("samp")), "samp", 0, 0), axis=0
+    )
     coef = collected[:systems_count].reshape(FOLDS, SHRINK, width, traits_count)
     coef_flat = coef.transpose(2, 0, 1, 3).reshape(width, FOLDS * SHRINK * traits_count)
     shift = jnp.einsum("v,klvt->klt", mean, coef.astype(jnp.float32), precision=HIGH)

time: 1100 us -> 1070 us (0.973)
  waiting for transfers between devices: 80.8 us -> 33.2 us
    all_gather x1 -> x0, waiting for transfers between devices: 76.2 us -> none  [shards(): collected = lax.all_gather(owned, 'samp', axis=0, tiled=True)]
    all_to_all x0 -> x1, waiting for transfers between devices: none -> 28.5 us  [shards(): lax.all_to_all(jnp.stack([owned] * lax.axis_size('samp')), 'samp', 0, 0)]
where the time goes in v1:
time: 1070 us; the launch traced here: 1060 us
  blocking collectives  749 us (70%)
  other arithmetic  198 us (19%)
  waiting for transfers between devices  33.2 us (3%)
  matrix products  27.3 us (3%)
  local copies, waits for them, and re-layouts  19.8 us (2%)
  between operations  19.1 us (2%)
  starting transfers between devices  13.8 us (1%)
    psum x1, blocking collectives, shards(): lax.psum((gram, sums, cross, counts, trait_sums), 'samp')  250 us
    psum x1, blocking collectives, shards(): fold_grams, fold_cross = lax.psum((fold_grams, fold_cross), 'samp')  245 us
    psum x1, blocking collectives, shards(): lax.psum((jnp.sum(blended, axis=-1), jnp.sum(blended * blended, axis=-1))...  129 us
    psum x1, blocking collectives, shards(): lax.psum((jnp.sum(level_pred, axis=-1), jnp.sum(level_pred * level_pred,...  126 us
    another operation x18, other arithmetic, solve_batch(): factors = jnp.linalg.cholesky(systems)  116 us
    another operation x6, other arithmetic, solve_single(): return jax.scipy.linalg.cho_solve((factor, True), right_side)  70.5 us
    all_to_all x1, waiting for transfers between devices, shards(): lax.all_to_all(jnp.stack([owned] * lax.axis_size('samp')), 'samp', 0, 0)  28.5 us
  transfers between devices with their start and end apart: 3, of which 2 were waited for; matrix products, arithmetic and copies ran while one was open for 0% of the time, Pallas kernels for 0%

profile of v1, /device:TPU:1, one launch (start us, length us, event | category | flops | bytes accessed | tf_op | source)
XLA Modules:
  0.0 1060.5 jit_solution(13947448492516772073)
XLA Ops:
  7.2 0.8 convert_bitcast_fusion
  8.0 3.0 fusion.4
  11.0 1.3 fusion.25
  12.3 3.0 fusion.3
  15.5 1.7 fusion.2
  17.4 1.8 fusion.1
  19.3 1.7 fusion
  21.2 0.7 copy-done.5
  22.4 250.1 %all-reduce.4 = (f32[5,512]{1,0:T(8,128)S(1)}, f32[5]{0:T(128)S(1)}, f32[5,16]{1,0:T(8,128)S(1)}) all-reduce(f32[5,512]{1,0:T(8,128)S(1)} %fusion.112, f32[5]{0:T(128)S(1)} %convert_reduce_fusion, f32[5,16]{1,0:T(8,128)S(1)} %fusion.96), channel_id=1, replica_groups=mesh['samp'=64,'blk'=4] {'samp'}, use_global_device_ids=true, to_apply=%region_5.0 | all-reduce | flops 2645 | bytes 21160 | tf_op jit(solution)/shard_map/psum | solution.py:42
  275.0 0.6 fusion.113
  276.2 3.3 reduce_sum.128
  279.5 5.0 gather_fusion
  285.1 2.3 fusion.38
  288.0 1.0 copy-done.2
  289.0 11.7 %custom-call.57 = f32[1,128,128]{2,1,0:T(8,128)S(1)} custom-call(f32[1,128,128]{2,1,0:T(8,128)S(1)} %cholesky.302), custom_call_target="Cholesky" | custom-call | tf_op jit(solution)/shard_map/while/body/eval_jaxpr/jit(cholesky)/cholesky | solution.py:14
  300.8 9.8 custom-call.58
  310.7 1.2 fusion.66
  312.0 1.2 fusion.14
  313.3 11.7 %custom-call.59 = f32[1,128,128]{2,1,0:T(8,128)S(1)} custom-call(f32[1,128,128]{2,1,0:T(8,128)S(1)} %cholesky.306), custom_call_target="Cholesky" | custom-call | tf_op jit(solution)/shard_map/while/body/eval_jaxpr/jit(cholesky)/cholesky | solution.py:14
  325.3 10.0 custom-call.60
  335.6 1.5 fusion.16
  337.1 11.7 %custom-call.61 = f32[1,128,128]{2,1,0:T(8,128)S(1)} custom-call(f32[1,128,128]{2,1,0:T(8,128)S(1)} %cholesky.311), custom_call_target="Cholesky" | custom-call | tf_op jit(solution)/shard_map/while/body/eval_jaxpr/jit(cholesky)/cholesky | solution.py:14
  349.0 9.8 custom-call.62
  359.1 1.3 fusion.19
  360.4 11.9 %custom-call.63 = f32[1,128,128]{2,1,0:T(8,128)S(1)} custom-call(f32[1,128,128]{2,1,0:T(8,128)S(1)} %fusion.19), custom_call_target="Cholesky" | custom-call | tf_op jit(solution)/shard_map/while/body/eval_jaxpr/jit(cholesky)/cholesky | solution.py:14
  372.5 0.7 compare_reduce_fusion.2
  373.2 0.6 compare_reduce_fusion.1
  373.8 0.7 compare_reduce_fusion.3
  377.2 8.9 while.1
  377.9 1.4 constant_dynamic-slice_fusion.8
  380.1 1.4 constant_dynamic-slice_fusion.8
  382.3 1.4 constant_dynamic-slice_fusion.8
  384.6 1.4 constant_dynamic-slice_fusion.8
  386.1 39.3 %custom-call.64 = f32[1,4,128,128]{2,3,1,0:T(8,128)S(1)} custom-call(f32[1,4,128,128]{3,2,1,0:T(8,128)S(1)} %bitcast.391), custom_call_target="InvertDiagBlocksLowerTriangular" | custom-call | tf_op jit(solution)/shard_map/while/body/eval_jaxpr/vmap(jit(_cho_solve))/triangular_solve | solution.py:17
  428.5 1.1 stack.38
  429.7 9.6 all-to-all-start
  439.3 28.5 %all-to-all-done = bf16[64,1,512,16]{2,3,1,0:T(8,128)(2,1)S(1)} async-done(((bf16[64,1,512,16]{2,3,1,0:T(8,128)(2,1)}), bf16[64,1,512,16]{2,3,1,0:T(8,128)(2,1)S(1)}, u32[]{:S(2)}, u32[]{:S(2)}) %all-to-all-start) | async-done | bytes 1048608 | tf_op jit(solution)/shard_map/all_to_all | solution.py:89
  467.8 1.5 fusion.47
  470.0 125.6 %all-reduce.3 = (f32[5,16]{1,0:T(8,128)S(1)}, f32[5,16]{1,0:T(8,128)S(1)}) all-reduce(f32[5,16]{1,0:T(8,128)S(1)} %get-tuple-element.90, f32[5,16]{1,0:T(8,128)S(1)} %get-tuple-element.89), channel_id=1, replica_groups=mesh['samp'=64,'blk'=4] {'samp'}, use_global_device_ids=true, to_apply=%region_23.24 | all-reduce | flops 160 | bytes 1280 | tf_op jit(solution)/shard_map/psum | solution.py:100
  596.2 0.9 copy.85
  597.1 4.2 all-to-all-start.1
  601.9 4.6 all-to-all-done.1
  607.2 1.4 fusion.11
  608.6 244.7 %all-reduce.2 = (f32[5,4,20,20]{3,2,0,1:T(8,128)S(1)}, f32[5,4,20]{2,0,1:T(8,128)S(1)}) all-reduce(f32[5,4,20,20]{3,2,0,1:T(8,128)S(1)} %fusion.11, f32[5,4,20]{2,0,1:T(8,128)S(1)} %fusion.61), channel_id=1, replica_groups=mesh['samp'=64,'blk'=4] {'samp'}, use_global_device_ids=true, to_apply=%region_24.25 | all-reduce | flops 8400 | bytes 67200 | tf_op jit(solution)/shard_map/psum | solution.py:111
  853.8 36.7 %custom-call.65 = f32[20,20,20]{2,1,0:T(8,128)S(1)} custom-call(f32[20,20,20]{2,1,0:T(8,128)S(1)} %fusion.54), custom_call_target="Cholesky" | custom-call | tf_op jit(solution)/shard_map/jit(cholesky)/cholesky | solution.py:14
  890.8 30.9 %custom-call.66 = f32[20,1,20,20]{2,3,1,0:T(8,128)S(1)} custom-call(f32[20,1,20,20]{3,2,1,0:T(8,128)S(1)} %select_bitcast_fusion), custom_call_target="InvertDiagBlocksLowerTriangular" | custom-call | tf_op jit(solution)/shard_map/vmap(jit(_cho_solve))/triangular_solve | solution.py:17
  923.1 129.1 %all-reduce.1 = (f32[4]{0:T(128)S(1)}, f32[4]{0:T(128)S(1)}) all-reduce(f32[4]{0:T(128)S(1)} %get-tuple-element.92, f32[4]{0:T(128)S(1)} %get-tuple-element.91), channel_id=1, replica_groups=mesh['samp'=64,'blk'=4] {'samp'}, use_global_device_ids=true, to_apply=%region_31.32 | all-reduce | flops 8 | bytes 64 | tf_op jit(solution)/shard_map/psum | solution.py:122
  1052.8 0.7 multiply_bitcast_fusion.1
  (126 shorter events, 16.8 us)
Async XLA Ops:
  7.2 8.2 copy-start
  7.2 8.1 copy-start.3
  7.2 269.0 %all-reduce.8.cloned.1.call-start = ((), (), s32[]{:S(2)}) async-start(), calls=%async_computation.2 | async-start | bytes 10813440 | tf_op jit(solution)/shard_map/psum | solution.py:42
  19.1 2.8 copy-start.6
  19.2 255.8 %copy-start.7 = (f32[5]{0:T(128)S(1)}, f32[5]{0:T(128)}, u32[]{:S(2)}) copy-start(f32[5]{0:T(128)} %constant.327) | copy-start | bytes 64
  21.2 0.7 copy-start.5
  288.0 1.0 copy-start.2
  289.0 136.5 %copy-start.4 = (f32[5,16,512]{2,1,0:T(8,128)S(1)}, f32[5,16,512]{2,1,0:T(8,128)}, u32[]{:S(2)}) copy-start(f32[5,16,512]{2,1,0:T(8,128)} %get-tuple-element.116) | copy-start | bytes 491524
  429.7 38.1 %all-to-all-start = ((bf16[64,1,512,16]{2,3,1,0:T(8,128)(2,1)}), bf16[64,1,512,16]{2,3,1,0:T(8,128)(2,1)S(1)}, u32[]{:S(2)}, u32[]{:S(2)}) async-start(bf16[64,1,512,16]{2,3,1,0:T(8,128)(2,1)} %stack.38), calls=%async_computation | async-start | bytes 2097152 | tf_op jit(solution)/shard_map/all_to_all | solution.py:89
  597.1 9.4 all-to-all-start.1
  606.6 446.8 %copy-start.1 = (f32[4,1,5,4,640]{4,3,2,0,1:T(4,128)}, f32[4,1,5,4,640]{4,3,2,0,1:T(4,128)S(1)}, u32[]{:S(2)}) copy-start(f32[4,1,5,4,640]{4,3,2,0,1:T(4,128)S(1)} %copy.143) | copy-start | bytes 614404
Sparse Core Ops, SparseCore 0:
  22.0 201.1 all-reduce.7
